TPU v7x, 128 devices: a whole 4x4x4 slice. The times are simulated.
128 devices in a mesh: src: 16 (over x_lo, z, core), loop: 8 (over x_hi, y).
Axes of the slice: x: 4 (x_hi: 2, x_lo: 2; x = x_hi * 2 + x_lo), y: 4, z: 4, core: 2. Of those that a mesh axis runs over, the one named last changes fastest.
Arguments:
- sources: bfloat16 [65536, 768], P(('src', 'loop')), may hold values from -48 to 48
- log_a: float32 [65536], P(('src', 'loop')), may hold values from -3 to 0
- targets: bfloat16 [128, 512, 768], P('src'), may hold values from -6 to 6
- g_old: bfloat16 [128, 512], P('src'), may hold values from -2.5 to 2.5
- log_b: float32 [128, 512], P('src'), may hold values from -3 to 0
- tile_ids: int32 [128, 16, 2], P(('src', 'loop')), may hold values from 0 to 127, as said below
- live_count: int32 [128, 16], P(('src', 'loop')), may hold values from 1 to 2, as said below
Outputs:
- f_new: float32 [65536], P(('src', 'loop'))
- g_new: float32 [128, 512], P('src')
Inputs may be any that keep to these rules, and one draw needn't show every extreme that they name: `tile_ids`: tile ids of one device for index o of src lie in o * 8 to (o + 1) * 8 - 1 and are distinct within that group of 2 slots; every tile is in use in some device's list. `live_count`: every index of src has a full group of 2 slots in use in some device's list.
All inputs are finite; a program needn't handle non-finite values.
Results may differ from a plain program's by a relative error of at most 0.0003.
Values may be sent and summed in bfloat16 or wider, within the bound.
No kernel may reach another device: no remote copies, remote signals or barrier semaphores. Data moves between devices by JAX's collectives and lax.ppermute only.
A program may use at most 128 MiB of HBM per device.

v0:
```python
import math
import jax
import jax.numpy as jnp
from jax import lax
from jax.sharding import PartitionSpec as P

EPSILON = 0.1
VERY_LOW = -1e30


def similarity(rows_bf, fetched):
    kernel = jnp.einsum("rd,ctd->rct", rows_bf, fetched, preferred_element_type=jnp.float32)
    return kernel / math.sqrt(rows_bf.shape[1])


def row_part(rows_bf, fetched, potential, live_slots):
    kernel = similarity(rows_bf, fetched)
    logits = (potential.astype(jnp.float32)[None] + kernel) / EPSILON
    logits = jnp.where(live_slots[None, :, None], logits, VERY_LOW)
    top = jnp.max(logits, axis=(1, 2))
    total = jnp.sum(jnp.exp(logits - top[:, None, None]), axis=(1, 2))
    return (top, total)


def col_part(rows_bf, row_potential, fetched, live_slots):
    kernel = similarity(rows_bf, fetched)
    logits = (row_potential[:, None, None] + kernel) / EPSILON
    top = jnp.max(logits, axis=0)
    total = jnp.sum(jnp.exp(logits - top[None]), axis=0)
    top = jnp.where(live_slots[:, None], top, VERY_LOW)
    total = jnp.where(live_slots[:, None], total, 0.0)
    return (top, total)


def local(sources, log_a, targets, g_old, log_b, tile_ids, live_count):
    tiles_own = targets.shape[0]
    width = targets.shape[1]
    slots_per = tile_ids.shape[2]
    me = lax.axis_index("src")
    rows_all = lax.all_gather(sources, "src")
    log_a_all = lax.all_gather(log_a, "src")
    ids_all = lax.all_gather(tile_ids[0], "src")
    live_all = lax.all_gather(live_count[0], "src")
    my_ids = lax.dynamic_index_in_dim(ids_all, me, 1, False) - me * tiles_own
    my_count = lax.dynamic_index_in_dim(live_all, me, 1, False)
    live_slots = jnp.arange(slots_per, dtype=jnp.int32)[None, :] < my_count[:, None]

    def rows_of(item):
        rows_bf, ids, live = item
        return row_part(rows_bf, targets[ids], g_old[ids], live)

    row_top, row_total = lax.map(rows_of, (rows_all, my_ids, live_slots))
    top = lax.pmax(row_top, "src")
    total = lax.psum(row_total * jnp.exp(row_top - top), "src")
    f_all = EPSILON * log_a_all - EPSILON * (top + jnp.log(total))
    f_new = lax.dynamic_index_in_dim(f_all, me, 0, False)

    def cols_of(item):
        rows_bf, f_rows, ids, live = item
        return col_part(rows_bf, f_rows, targets[ids], live)

    col_top, col_total = lax.map(cols_of, (rows_all, f_all, my_ids, live_slots))
    flat_ids = my_ids.reshape(-1)
    flat_top = col_top.reshape(-1, width)
    flat_total = col_total.reshape(-1, width)
    onehot = flat_ids[:, None] == jnp.arange(tiles_own, dtype=jnp.int32)[None, :]
    tile_top = jnp.max(jnp.where(onehot[:, :, None], flat_top[:, None, :], VERY_LOW), axis=0)
    scaled = flat_total[:, None, :] * jnp.exp(
        jnp.minimum(flat_top[:, None, :] - tile_top[None], 0.0)
    )
    tile_total = jnp.sum(jnp.where(onehot[:, :, None], scaled, 0.0), axis=0)
    all_top = lax.pmax(tile_top, "loop")
    all_total = lax.psum(tile_total * jnp.exp(tile_top - all_top), "loop")
    g_new = EPSILON * log_b - EPSILON * (all_top + jnp.log(all_total))
    return (f_new, g_new)


def solution(mesh):
    return jax.shard_map(
        local,
        mesh=mesh,
        in_specs=(
            P(("src", "loop"), None),
            P(("src", "loop")),
            P("src", None, None),
            P("src", None),
            P("src", None),
            P(("src", "loop"), None, None),
            P(("src", "loop"), None),
        ),
        out_specs=(P(("src", "loop")), P("src", None)),
        check_vma=False,
    )
```

profile of v0, /device:TPU:0, one launch (start us, length us, event | category | flops | bytes accessed | tf_op | source)
XLA Modules:
  0.0 501.2 jit_solution(8894537044187313514)
XLA Ops:
  7.9 21.4 %all_gather.21 = s32[16,16,2]{1,2,0:T(2,128)S(1)} all-gather(s32[1,16,2]{1,2,0:T(2,128)} %param.16), channel_id=1, replica_groups=mesh['src'=16,'loop'=8] {'src'}, dimensions={0}, use_global_device_ids=true | all-gather | bytes 2176 | tf_op jit(solution)/shard_map/all_gather | solution.py:42
  30.1 17.0 %all-gather.3 = s32[16,1,16]{2,1,0:T(1,128)S(1)} all-gather(s32[1,1,16]{2,1,0:T(1,128)} %bitcast.87), channel_id=1, replica_groups=mesh['src'=16,'loop'=8] {'src'}, dimensions={0}, use_global_device_ids=true | all-gather | bytes 1088 | tf_op jit(solution)/shard_map/all_gather | solution.py:43
  47.5 18.6 %all-gather.2 = f32[16,1,512]{2,1,0:T(1,128)S(1)} all-gather(f32[1,1,512]{2,1,0:T(1,128)} %bitcast.85), channel_id=2, replica_groups=mesh['src'=16,'loop'=8] {'src'}, dimensions={0}, use_global_device_ids=true | all-gather | bytes 34816 | tf_op jit(solution)/shard_map/all_gather | solution.py:41
  66.2 18.0 %all-gather.6.cloned.1.call-done = bf16[8192,768]{1,0:T(8,128)(2,1)} async-done(((bf16[512,768]{1,0:T(8,128)(2,1)}), bf16[8192,768]{1,0:T(8,128)(2,1)}) %all-gather.6.cloned.1.call-update) | async-done | bytes 12582928 | tf_op jit(solution)/shard_map/all_gather | solution.py:40
  84.2 120.7 %while.24 = (s32[]{:T(128)}, f32[16,512]{1,0:T(8,128)S(1)}, f32[16,512]{1,0:T(8,128)S(1)}, pred[16,2]{1,0:T(8,128)(4,1)S(1)}, s32[16,2]{1,0:T(8,128)S(1)}, /*ind...) while((s32[]{:T(128)}, f32[16,512]{1,0:T(8,128)S(1)}, ...), condition=%wide.region_3.4_spmd, body=%wide.region_0.3_spmd.sunk | while | flops 808977408 | bytes 9732271 | solution.py:52
  85.5 3.4 gather_fusion
  93.1 3.4 gather_fusion
  100.6 3.4 gather_fusion
  108.1 3.4 gather_fusion
  115.7 3.4 gather_fusion
  123.2 3.4 gather_fusion
  130.8 3.4 gather_fusion
  138.3 3.4 gather_fusion
  145.9 3.4 gather_fusion
  153.4 3.4 gather_fusion
  161.0 3.4 gather_fusion
  168.5 3.4 gather_fusion
  176.1 3.4 gather_fusion
  204.9 55.7 %pmax.14 = f32[16,512]{1,0:T(8,128)S(1)} all-reduce(f32[16,512]{1,0:T(8,128)S(1)} %get-tuple-element.88), channel_id=1, replica_groups=mesh['src'=16,'loop'=8] {'src'}, use_global_device_ids=true, to_apply=%region_4.5 | all-reduce | flops 8192 | bytes 65536 | tf_op jit(solution)/shard_map/pmax | solution.py:53
  260.7 52.9 %psum.14 = f32[16,512]{1,0:T(8,128)S(1)} all-reduce(f32[16,512]{1,0:T(8,128)S(1)} %exponential_multiply_fusion), channel_id=1, replica_groups=mesh['src'=16,'loop'=8] {'src'}, use_global_device_ids=true, to_apply=%region_5.6 | all-reduce | flops 8192 | bytes 65536 | tf_op jit(solution)/shard_map/psum | solution.py:54
  314.2 101.2 %while.25 = (s32[]{:T(128)}, f32[16,2,512]{2,1,0:T(2,128)S(1)}, f32[16,2,512]{2,1,0:T(2,128)S(1)}, pred[16,2]{1,0:T(8,128)(4,1)S(1)}, f32[16,512]{1,0:T(8,128)S(...) while((s32[]{:T(128)}, f32[16,2,512]{2,1,0:T(2,128)S(1)}, ...), condition=%wide.region_9.10_spmd, body=%wide.region_6.9_spmd.sunk | while | flops 810025984 | bytes 9740957 | solution.py:62
  314.2 3.4 gather_fusion.2
  320.6 3.4 gather_fusion.2
  326.9 3.4 gather_fusion.2
  339.5 3.4 gather_fusion.2
  352.2 3.4 gather_fusion.2
  364.8 3.4 gather_fusion.2
  377.5 3.4 gather_fusion.2
  390.1 3.4 gather_fusion.2
  402.8 3.4 gather_fusion.2
  415.6 41.4 %pmax.15 = f32[8,512]{1,0:T(8,128)S(1)} all-reduce(f32[8,512]{1,0:T(8,128)S(1)} %select_reduce_fusion.1), channel_id=1, replica_groups=mesh['src'=16,'loop'=8] {'loop'}, use_global_device_ids=true, to_apply=%region_11.12 | all-reduce | flops 4096 | bytes 32768 | tf_op jit(solution)/shard_map/pmax | solution.py:72
  457.1 36.6 %psum.15 = f32[8,512]{1,0:T(8,128)S(1)} all-reduce(f32[8,512]{1,0:T(8,128)S(1)} %exponential_multiply_fusion.1), channel_id=1, replica_groups=mesh['src'=16,'loop'=8] {'loop'}, use_global_device_ids=true, to_apply=%region_13.14 | all-reduce | flops 4096 | bytes 32768 | tf_op jit(solution)/shard_map/psum | solution.py:73
  (291 shorter events, 148.3 us)
Async XLA Ops:
  7.2 77.0 %all-gather.6.cloned.1.call-start = ((), (), s32[]{:S(2)}) async-start(), calls=%async_computation | async-start | bytes 13369344 | tf_op jit(solution)/shard_map/all_gather | solution.py:40
  314.2 179.6 %copy-start = (f32[8,512]{1,0:T(8,128)S(1)}, f32[8,512]{1,0:T(8,128)}, u32[]{:S(2)}) copy-start(f32[8,512]{1,0:T(8,128)} %param.15) | copy-start | bytes 49156
Sparse Core Ops, SparseCore 0:
  9.7 74.4 all-gather.5
where the time goes:
time: 505 us; the launch traced here: 501 us
  blocking collectives  244 us (48%)
  local copies, waits for them, and re-layouts  134 us (27%)
  matrix products  70.9 us (14%)
  waiting for transfers between devices  18.7 us (4%)
  other arithmetic  18.2 us (4%)
  between operations  14.1 us (3%)
    gather x32, local copies, waits for them, and re-layouts, rows_of(): return row_part(rows_bf, targets[ids], g_old[ids], live)  75.1 us
    dot_general x32, matrix products, similarity(): jnp.einsum('rd,ctd->rct', rows_bf, fetched, preferred_element_type=jnp.fl...  70.9 us
    pmax x1, blocking collectives, local(): top = lax.pmax(row_top, 'src')  55.7 us
    gather x16, local copies, waits for them, and re-layouts, cols_of(): return col_part(rows_bf, f_rows, targets[ids], live)  54.9 us
    psum x1, blocking collectives, local(): total = lax.psum(row_total * jnp.exp(row_top - top), 'src')  52.9 us
    pmax x1, blocking collectives, local(): all_top = lax.pmax(tile_top, 'loop')  41.4 us
    psum x1, blocking collectives, local(): all_total = lax.psum(tile_total * jnp.exp(tile_top - all_top), 'loop')  36.6 us
    all_gather x1, blocking collectives, local(): ids_all = lax.all_gather(tile_ids[0], 'src')  21.4 us
  transfers between devices with their start and end apart: 1, of which 1 were waited for; matrix products, arithmetic and copies ran while one was open for 0% of the time, Pallas kernels for 0%

commit v1 on v0

--- a/solution.py
+++ b/solution.py
@@ -70,7 +70,7 @@
     )
     tile_total = jnp.sum(jnp.where(onehot[:, :, None], scaled, 0.0), axis=0)
     all_top = lax.pmax(tile_top, "loop")
-    all_total = lax.psum(tile_total * jnp.exp(tile_top - all_top), "loop")
+    all_total = jnp.sum(lax.all_gather(tile_total * jnp.exp(tile_top - all_top), "loop"), axis=0)
     g_new = EPSILON * log_b - EPSILON * (all_top + jnp.log(all_total))
     return (f_new, g_new)
 

time: 505 us -> 502 us (level)
    psum x1 -> x0, blocking collectives: 36.6 us -> none  [local(): all_total = lax.psum(tile_total * jnp.exp(tile_top - all_top), 'loop')]
    all_gather x0 -> x1, blocking collectives: none -> 34.2 us  [local(): lax.all_gather(tile_total * jnp.exp(tile_top - all_top), 'loop')]
where the time goes in v1:
time: 502 us; the launch traced here: 499 us
  blocking collectives  241 us (48%)
  local copies, waits for them, and re-layouts  134 us (27%)
  matrix products  70.9 us (14%)
  waiting for transfers between devices  18.7 us (4%)
  other arithmetic  18.2 us (4%)
  between operations  14.1 us (3%)
    gather x32, local copies, waits for them, and re-layouts, rows_of(): return row_part(rows_bf, targets[ids], g_old[ids], live)  75.1 us
    dot_general x32, matrix products, similarity(): jnp.einsum('rd,ctd->rct', rows_bf, fetched, preferred_element_type=jnp.fl...  70.9 us
    pmax x1, blocking collectives, local(): top = lax.pmax(row_top, 'src')  55.7 us
    gather x16, local copies, waits for them, and re-layouts, cols_of(): return col_part(rows_bf, f_rows, targets[ids], live)  54.9 us
    psum x1, blocking collectives, local(): total = lax.psum(row_total * jnp.exp(row_top - top), 'src')  52.9 us
    pmax x1, blocking collectives, local(): all_top = lax.pmax(tile_top, 'loop')  41.4 us
    all_gather x1, blocking collectives, local(): lax.all_gather(tile_total * jnp.exp(tile_top - all_top), 'loop')  34.2 us
    all_gather x1, blocking collectives, local(): ids_all = lax.all_gather(tile_ids[0], 'src')  21.4 us
  transfers between devices with their start and end apart: 1, of which 1 were waited for; matrix products, arithmetic and copies ran while one was open for 0% of the time, Pallas kernels for 0%

profile of v1, /device:TPU:0, one launch (start us, length us, event | category | flops | bytes accessed | tf_op | source)
XLA Modules:
  0.0 498.8 jit_solution(13316229181448420800)
XLA Ops:
  7.9 21.4 %all_gather.27 = s32[16,16,2]{1,2,0:T(2,128)S(1)} all-gather(s32[1,16,2]{1,2,0:T(2,128)} %param.16), channel_id=1, replica_groups=mesh['src'=16,'loop'=8] {'src'}, dimensions={0}, use_global_device_ids=true | all-gather | bytes 2176 | tf_op jit(solution)/shard_map/all_gather | solution.py:42
  30.1 17.0 %all-gather.4 = s32[16,1,16]{2,1,0:T(1,128)S(1)} all-gather(s32[1,1,16]{2,1,0:T(1,128)} %bitcast.89), channel_id=1, replica_groups=mesh['src'=16,'loop'=8] {'src'}, dimensions={0}, use_global_device_ids=true | all-gather | bytes 1088 | tf_op jit(solution)/shard_map/all_gather | solution.py:43
  47.5 18.6 %all-gather.3 = f32[16,1,512]{2,1,0:T(1,128)S(1)} all-gather(f32[1,1,512]{2,1,0:T(1,128)} %bitcast.87), channel_id=2, replica_groups=mesh['src'=16,'loop'=8] {'src'}, dimensions={0}, use_global_device_ids=true | all-gather | bytes 34816 | tf_op jit(solution)/shard_map/all_gather | solution.py:41
  66.2 18.0 %all-gather.7.cloned.1.call-done = bf16[8192,768]{1,0:T(8,128)(2,1)} async-done(((bf16[512,768]{1,0:T(8,128)(2,1)}), bf16[8192,768]{1,0:T(8,128)(2,1)}) %all-gather.7.cloned.1.call-update) | async-done | bytes 12582928 | tf_op jit(solution)/shard_map/all_gather | solution.py:40
  84.2 120.7 %while.24 = (s32[]{:T(128)}, f32[16,512]{1,0:T(8,128)S(1)}, f32[16,512]{1,0:T(8,128)S(1)}, pred[16,2]{1,0:T(8,128)(4,1)S(1)}, s32[16,2]{1,0:T(8,128)S(1)}, /*ind...) while((s32[]{:T(128)}, f32[16,512]{1,0:T(8,128)S(1)}, ...), condition=%wide.region_3.4_spmd, body=%wide.region_0.3_spmd.sunk | while | flops 808977408 | bytes 9732271 | solution.py:52
  85.5 3.4 gather_fusion
  93.1 3.4 gather_fusion
  100.6 3.4 gather_fusion
  108.1 3.4 gather_fusion
  115.7 3.4 gather_fusion
  123.2 3.4 gather_fusion
  130.8 3.4 gather_fusion
  138.3 3.4 gather_fusion
  145.9 3.4 gather_fusion
  153.4 3.4 gather_fusion
  161.0 3.4 gather_fusion
  168.5 3.4 gather_fusion
  176.1 3.4 gather_fusion
  204.9 55.7 %pmax.14 = f32[16,512]{1,0:T(8,128)S(1)} all-reduce(f32[16,512]{1,0:T(8,128)S(1)} %get-tuple-element.88), channel_id=1, replica_groups=mesh['src'=16,'loop'=8] {'src'}, use_global_device_ids=true, to_apply=%region_4.5 | all-reduce | flops 8192 | bytes 65536 | tf_op jit(solution)/shard_map/pmax | solution.py:53
  260.7 52.9 %psum.7 = f32[16,512]{1,0:T(8,128)S(1)} all-reduce(f32[16,512]{1,0:T(8,128)S(1)} %exponential_multiply_fusion), channel_id=1, replica_groups=mesh['src'=16,'loop'=8] {'src'}, use_global_device_ids=true, to_apply=%region_5.6 | all-reduce | flops 8192 | bytes 65536 | tf_op jit(solution)/shard_map/psum | solution.py:54
  314.2 101.2 %while.25 = (s32[]{:T(128)}, f32[16,2,512]{2,1,0:T(2,128)S(1)}, f32[16,2,512]{2,1,0:T(2,128)S(1)}, pred[16,2]{1,0:T(8,128)(4,1)S(1)}, f32[16,512]{1,0:T(8,128)S(...) while((s32[]{:T(128)}, f32[16,2,512]{2,1,0:T(2,128)S(1)}, ...), condition=%wide.region_9.10_spmd, body=%wide.region_6.9_spmd.sunk | while | flops 810025984 | bytes 9740957 | solution.py:62
  314.2 3.4 gather_fusion.2
  320.6 3.4 gather_fusion.2
  326.9 3.4 gather_fusion.2
  339.5 3.4 gather_fusion.2
  352.2 3.4 gather_fusion.2
  364.8 3.4 gather_fusion.2
  377.5 3.4 gather_fusion.2
  390.1 3.4 gather_fusion.2
  402.8 3.4 gather_fusion.2
  415.6 41.4 %pmax.15 = f32[8,512]{1,0:T(8,128)S(1)} all-reduce(f32[8,512]{1,0:T(8,128)S(1)} %select_reduce_fusion.1), channel_id=1, replica_groups=mesh['src'=16,'loop'=8] {'loop'}, use_global_device_ids=true, to_apply=%region_11.12 | all-reduce | flops 4096 | bytes 32768 | tf_op jit(solution)/shard_map/pmax | solution.py:72
  457.1 34.2 %all-gather.2 = f32[64,512]{1,0:T(8,128)S(1)} all-gather(f32[8,512]{1,0:T(8,128)S(1)} %exponential_multiply_fusion.1), channel_id=4, replica_groups=mesh['src'=16,'loop'=8] {'loop'}, dimensions={0}, use_global_device_ids=true | all-gather | bytes 147456 | tf_op jit(solution)/shard_map/all_gather | solution.py:73
  (292 shorter events, 148.3 us)
Async XLA Ops:
  7.2 77.0 %all-gather.7.cloned.1.call-start = ((), (), s32[]{:S(2)}) async-start(), calls=%async_computation | async-start | bytes 13369344 | tf_op jit(solution)/shard_map/all_gather | solution.py:40
  314.2 177.2 %copy-start = (f32[8,512]{1,0:T(8,128)S(1)}, f32[8,512]{1,0:T(8,128)}, u32[]{:S(2)}) copy-start(f32[8,512]{1,0:T(8,128)} %param.15) | copy-start | bytes 49156
Sparse Core Ops, SparseCore 0:
  9.7 74.4 all-gather.6
